TPU v7x, 512 devices: a whole 4x8x8 slice. The times are simulated.
512 devices in a mesh: dp: 32 (over y, x), section: 4 (over z_hi), space: 4 (over z_lo, core).
Axes of the slice: x: 4, y: 8, z: 8 (z_hi: 4, z_lo: 2; z = z_hi * 2 + z_lo), core: 2. Of those that a mesh axis runs over, the one named last changes fastest.
Arguments:
- images: bfloat16 [64, 4, 64, 256], P('dp', 'space'), may hold values from -6 to 6
- steps: int32 [64], P('dp'), may hold values from 0 to 999
- out_grad: bfloat16 [64, 4, 64, 256], P('dp', 'space'), may hold values from -0.125 to 0.125
- conv_weight: bfloat16 [4, 3, 3, 256, 256], P('section'), may hold values from -0.125 to 0.125
- gn_gain: float32 [4, 256], P('section'), may hold values from 0.5 to 2
- emb_weight: bfloat16 [4, 256, 512], P('section'), may hold values from -0.375 to 0.375
Outputs:
- grad_conv: float32 [4, 3, 3, 256, 256], P('section')
- grad_gain: float32 [4, 256], P('section')
- grad_emb: float32 [4, 256, 512], P('section')
All inputs are finite; a program needn't handle non-finite values.
Results may differ from a plain program's by a relative error of at most 0.0064.
Values may be sent and summed in bfloat16 or wider, within the bound.
No kernel may reach another device: no remote copies, remote signals or barrier semaphores. Data moves between devices by JAX's collectives and lax.ppermute only.
A program may use at most 64 MiB of HBM per device.

v0:
```python
import math
import jax
import jax.numpy as jnp
from jax import lax
from jax.sharding import Mesh, PartitionSpec as P

G = 32
FREQ = 256
MICRO = 2
EPS = 1e-05


def from_behind(value, axis, steps):
    count = lax.axis_size(axis)
    initial, last = (max(0, -steps), min(count, count - steps))
    return lax.ppermute(value, axis, [(source, source + steps) for source in range(initial, last)])


def extended(shard, sides, width):
    for axis, dim in sides:
        size, length = (lax.axis_size(axis), shard.shape[dim])
        up = [(i, (i + 1) % size) for i in range(size - 1)]
        down = [(j, i) for i, j in up]
        last = lax.slice_in_dim(shard, length - width, length, axis=dim)
        initial = lax.slice_in_dim(shard, 0, width, axis=dim)
        before = lax.ppermute(last, axis, up)
        after = lax.ppermute(initial, axis, down)
        shard = jnp.concatenate([before, shard, after], axis=dim)
    return shard


def sinusoid(timesteps, feature_n):
    half_n = feature_n // 2
    freqs = jnp.exp(-math.log(10000.0) * jnp.arange(half_n, dtype=jnp.float32) / half_n)
    angles = timesteps.astype(jnp.float32)[:, None] * freqs[None, :]
    return jnp.concatenate([jnp.cos(angles), jnp.sin(angles)], axis=1)


def group_sums(tensor, groups):
    batch_n, height_n, width_n, channels = tensor.shape
    split = tensor.reshape(batch_n, height_n, width_n, groups, channels // groups)
    return (jnp.sum(split, axis=(1, 2, 4)), jnp.sum(split * split, axis=(1, 2, 4)))


def spread(values, channels):
    return jnp.repeat(values, channels // values.shape[1], axis=1)[:, None, None, :]


def normalize(tensor, first_sum, square_sum, gains, scales, shifts, cell_count):
    channels = tensor.shape[3]
    average = first_sum / cell_count
    inverse = lax.rsqrt(square_sum / cell_count - average * average + EPS)
    normed = (tensor - spread(average, channels)) * spread(inverse, channels) * gains
    return normed * (1.0 + scales[:, None, None, :]) + shifts[:, None, None, :]


def patches(padded, height_n, width_n):
    return jnp.concatenate(
        [
            padded[:, vertical : vertical + height_n, lateral : lateral + width_n, :]
            for vertical in range(3)
            for lateral in range(3)
        ],
        axis=3,
    )


def convolve(padded, matrix):
    batch_n, height_p, width_p, channels = padded.shape
    flat = patches(padded, height_p - 2, width_p - 2).reshape(-1, 9 * channels)
    return jnp.dot(flat, matrix, preferred_element_type=jnp.float32).reshape(
        batch_n, height_p - 2, width_p - 2, matrix.shape[1]
    )


def flip_weight(weight):
    channels = weight.shape[2]
    return jnp.transpose(weight[::-1, ::-1], (0, 1, 3, 2)).reshape(9 * channels, channels)


def silu_slope(pre_act):
    sigmoid_v = jax.nn.sigmoid(pre_act)
    return sigmoid_v * (1.0 + pre_act * (1.0 - sigmoid_v))


def pad_columns(tensor):
    return jnp.pad(tensor, ((0, 0), (0, 0), (1, 1), (0, 0)))


def pick(stacked, index):
    return lax.dynamic_index_in_dim(stacked, index, 0, keepdims=False)


def norm_backward(tensor, first_sum, square_sum, gains, scales, shifts, cell_count, d_pre):

    def mapping(tensor_v, first_v, square_v, gains_v, scales_v, shifts_v):
        return normalize(tensor_v, first_v, square_v, gains_v, scales_v, shifts_v, cell_count)

    _, pull_back = jax.vjp(mapping, tensor, first_sum, square_sum, gains, scales, shifts)
    return pull_back(d_pre)


def pad_both(tensor):
    return jnp.pad(tensor, ((0, 0), (1, 1), (1, 1), (0, 0)))


def group_blocks(channels):
    group = jnp.arange(channels) // (channels // G)
    return (group[:, None] == group[None, :]).astype(jnp.float32)


def over_groups(values, blocks):
    return jnp.dot(values, blocks, precision=lax.Precision.HIGHEST)


def normalize_spread(tensor, first_c, square_c, gains, scales, shifts, cell_count):
    average = first_c / cell_count
    inverse = lax.rsqrt(square_c / cell_count - average * average + EPS)
    normed = (tensor - average[:, None, None, :]) * inverse[:, None, None, :] * gains
    return normed * (1.0 + scales[:, None, None, :]) + shifts[:, None, None, :]


def conv_same(tensor, kernel):
    return lax.conv_general_dilated(
        tensor,
        kernel,
        (1, 1),
        ((1, 1), (1, 1)),
        dimension_numbers=("NHWC", "HWIO", "NHWC"),
        preferred_element_type=jnp.float32,
    )


def block_forward(inputs, flat_weight, gains, scales, shifts, cell_count):
    tensor = inputs.astype(jnp.float32)
    blocks = group_blocks(tensor.shape[3])
    first_c = over_groups(jnp.sum(tensor, axis=(1, 2)), blocks)
    square_c = over_groups(jnp.sum(tensor * tensor, axis=(1, 2)), blocks)
    pre_act = normalize_spread(tensor, first_c, square_c, gains, scales, shifts, cell_count)
    activation = jax.nn.silu(pre_act).astype(jnp.bfloat16)
    padded = pad_both(activation)
    output = (tensor + conv_same(activation, flat_weight)).astype(jnp.bfloat16)
    return (output, (first_c, square_c, padded))


def block_backward(upstream, inputs, saved, flipped, gains, scales, shifts, cell_count):
    first_c, square_c, _ = saved
    tensor = inputs.astype(jnp.float32)
    blocks = group_blocks(tensor.shape[3])
    pre_act = normalize_spread(tensor, first_c, square_c, gains, scales, shifts, cell_count)
    d_act = conv_same(upstream, flipped)
    d_pre = d_act * silu_slope(pre_act)

    def mapping(tensor_v, first_v, square_v, gains_v, scales_v, shifts_v):
        return normalize_spread(
            tensor_v, first_v, square_v, gains_v, scales_v, shifts_v, cell_count
        )

    _, pull_back = jax.vjp(mapping, tensor, first_c, square_c, gains, scales, shifts)
    d_tensor, d_first, d_square, d_gains, d_scales, d_shifts = pull_back(d_pre)
    d_first = over_groups(d_first, blocks)[:, None, None, :]
    d_square = over_groups(d_square, blocks)[:, None, None, :]
    d_tensor = d_tensor + d_first + 2.0 * tensor * d_square
    d_input = (upstream.astype(jnp.float32) + d_tensor).astype(jnp.bfloat16)
    return (d_input, (d_gains, d_scales, d_shifts))


def keep(flag, new, old):
    return jax.tree.map(lambda a, b: jnp.where(flag, a, b), new, old)


def per_device(images, steps, out_grad, conv_weight, gn_gain, emb_weight):
    section_count = lax.axis_size("section")
    section_no = lax.axis_index("section")
    images = lax.all_gather(images, "space", axis=1, tiled=True)
    out_grad = lax.all_gather(out_grad, "space", axis=1, tiled=True)
    row_count = images.shape[1]
    col_count = images.shape[2]
    channels = images.shape[3]
    cell_count = row_count * col_count * (channels // G)
    weight = conv_weight[0]
    flat_weight = weight
    flipped = jnp.transpose(weight[::-1, ::-1], (0, 1, 3, 2))
    gains = gn_gain[0]
    features = sinusoid(steps, FREQ)
    embedded = jnp.dot(features, emb_weight[0].astype(jnp.float32), precision=lax.Precision.HIGHEST)
    scales = embedded[:, :channels]
    shifts = embedded[:, channels:]
    last = section_count - 1
    carried = images
    kept = None
    for moment in range(section_count):
        inputs = images
        if moment > 0:
            inputs = lax.ppermute(carried, "section", [(moment - 1, moment)])
        if moment == last:
            inputs = (inputs.astype(jnp.float32) + skip.astype(jnp.float32)).astype(jnp.bfloat16)
        output, saved = block_forward(inputs, flat_weight, gains, scales, shifts, cell_count)
        if moment == 0:
            skip = lax.ppermute(output, "section", [(0, last)])
        state = (inputs, saved)
        kept = state if kept is None else keep(section_no == moment, state, kept)
        carried = output
    kept_in, kept_saved = kept
    carried = out_grad
    kept = None
    for moment in range(section_count):
        active = last - moment
        upstream = out_grad
        if moment > 0:
            upstream = lax.ppermute(carried, "section", [(active + 1, active)])
        if active == 0:
            upstream = (upstream.astype(jnp.float32) + skip_grad.astype(jnp.float32)).astype(
                jnp.bfloat16
            )
        d_input, pieces = block_backward(
            upstream, kept_in, kept_saved, flipped, gains, scales, shifts, cell_count
        )
        if moment == 0:
            skip_grad = lax.ppermute(d_input, "section", [(last, 0)])
        state = (upstream, pieces)
        kept = state if kept is None else keep(section_no == active, state, kept)
        carried = d_input
    kept_up, (d_gains, d_scales, d_shifts) = kept
    space_count = lax.axis_size("space")
    space_no = quarter_of(lax.axis_index("space"), space_count)
    patch_rows = 9 * channels // space_count
    flat_patch = patches(kept_saved[2], row_count, col_count).reshape(-1, 9 * channels)
    own_patch = lax.dynamic_slice_in_dim(flat_patch, space_no * patch_rows, patch_rows, axis=1)
    weight_grad = jnp.dot(
        own_patch.T, kept_up.reshape(-1, channels), preferred_element_type=jnp.float32
    )
    emb_rows = FREQ // space_count
    own_features = lax.dynamic_slice_in_dim(features, space_no * emb_rows, emb_rows, axis=1)
    emb_grad = jnp.dot(
        own_features.T,
        jnp.concatenate([d_scales, d_shifts], axis=1),
        precision=lax.Precision.HIGHEST,
    )
    return reduce_grads(weight_grad, d_gains, emb_grad)


def butterfly_scatter(flat, axis):
    count = lax.axis_size(axis)
    index = lax.axis_index(axis)
    step = 1
    while step < count:
        bit = index // step % 2
        half = flat.shape[0] // 2
        kept = lax.dynamic_slice_in_dim(flat, bit * half, half, 0)
        sent = lax.dynamic_slice_in_dim(flat, (1 - bit) * half, half, 0)
        flat = kept + lax.ppermute(sent, axis, [(j, j ^ step) for j in range(count)])
        step *= 2
    return flat


def butterfly_sum(flat, axis):
    count = lax.axis_size(axis)
    step = 1
    while step < count:
        flat = flat + lax.ppermute(flat, axis, [(j, j ^ step) for j in range(count)])
        step *= 2
    return flat


def butterfly_gather(flat, axis, steps):
    count = lax.axis_size(axis)
    index = lax.axis_index(axis)
    for step in steps:
        bit = index // step % 2
        got = lax.ppermute(flat, axis, [(j, j ^ step) for j in range(count)])
        length = flat.shape[0]
        joined = jnp.concatenate([flat, flat])
        flat = lax.dynamic_update_slice_in_dim(joined, got, (1 - bit) * length, 0)
    return flat


def descending(count):
    steps = []
    step = count // 2
    while step >= 1:
        steps.append(step)
        step //= 2
    return steps


def quarter_of(space_no, space_count):
    return space_no % 2 * (space_count // 2) + space_no // 2


def reduce_grads(weight_grad, gain_grad, emb_grad):
    channels = gain_grad.shape[0]
    parts = [weight_grad, emb_grad.reshape(-1, channels), gain_grad[None]]
    rows = sum((part.shape[0] for part in parts))
    devices = lax.axis_size("dx")
    padded_rows = -(-rows // (8 * devices)) * 8 * devices
    parts.append(jnp.zeros((padded_rows - rows, channels), jnp.float32))
    flat = jnp.concatenate(parts, axis=0)
    flat = butterfly_scatter(flat, "dx")
    flat = butterfly_sum(flat, "dy")
    flat = butterfly_gather(flat.astype(jnp.bfloat16), "dx", descending(lax.axis_size("dx")))
    space_count = lax.axis_size("space")
    flat = butterfly_gather(flat, "space", descending(space_count))
    flat = flat.reshape(space_count, padded_rows, channels).astype(jnp.float32)
    weight_rows = weight_grad.shape[0]
    emb_rows = emb_grad.size // channels
    conv = flat[:, :weight_rows].reshape(1, 3, 3, channels, channels)
    emb = flat[:, weight_rows : weight_rows + emb_rows].reshape(
        1, emb_grad.shape[0] * space_count, -1
    )
    gain = flat[0, weight_rows + emb_rows][None]
    return (conv, gain, emb)


def solution(mesh):
    dp_n = mesh.shape["dp"]
    dx_n = 4 if dp_n % 4 == 0 else 1
    mesh = Mesh(
        mesh.devices.reshape(dp_n // dx_n, dx_n, *mesh.devices.shape[1:]),
        ("dy", "dx", "section", "space"),
    )
    data = ("dy", "dx")
    in_specs = (
        P(data, "space", None, None),
        P(data),
        P(data, "space", None, None),
        P("section", None, None, None, None),
        P("section", None),
        P("section", None, None),
    )
    out_specs = (P("section", None, None, None, None), P("section", None), P("section", None, None))
    return jax.shard_map(
        per_device, mesh=mesh, in_specs=in_specs, out_specs=out_specs, check_vma=False
    )
```

profile of v0, /device:TPU:25, one launch (start us, length us, event | category | flops | bytes accessed | tf_op | source)
XLA Modules:
  0.0 192.3 jit_solution(9327620106959557601)
XLA Ops:
  0.7 7.5 %all_gather.6 = bf16[2,4,64,256]{3,2,0,1:T(8,128)(2,1)S(1)} all-gather(bf16[2,1,64,256]{3,2,0,1:T(8,128)(2,1)} %bitcast.164), channel_id=1, replica_groups=mesh['dy'=8,'dx'=4,'section'=4,'space'=4] {'space'}, dimensions={1}, use_global_device_ids=true | all-gather | bytes 327680 | tf_op jit(solution)/shard_map/all_gather | solution.py:175
  8.4 0.7 convert_element_type.101
  9.2 1.2 fusion.130
  10.9 1.2 fusion.221
  13.0 0.9 convolution_select_fusion.6
  14.5 5.8 %collective-permute-start = (bf16[2,4,64,256]{3,1,2,0:T(4,128)(2,1)S(1)}, bf16[2,4,64,256]{3,1,2,0:T(4,128)(2,1)S(1)}, u32[]{:S(2)}, u32[]{:S(2)}) collective-permute-start(bf16[2,4,64,256]{3,1,2,0:T(4,128)(2,1)S(1)} %fusion.79), channel_id=1, source_target_pairs={{0,4},{1,5},{2,6},{3,7},{16,20},{17,21},{18,22},{19,23},{32,36},{3... | collective-permute-start | bytes 786440 | tf_op jit(solution)/shard_map/ppermute | solution.py:195
  20.3 4.7 %collective-permute-start.3 = (bf16[2,4,64,256]{3,1,2,0:T(4,128)(2,1)S(1)}, bf16[2,4,64,256]{3,1,2,0:T(4,128)(2,1)S(1)}, u32[]{:S(2)}, u32[]{:S(2)}) collective-permute-start(bf16[2,4,64,256]{3,1,2,0:T(4,128)(2,1)S(1)} %fusion.79), channel_id=1, source_target_pairs={{0,12},{1,13},{2,14},{3,15},{16,28},{17,29},{18,30},{19,31},{32,44... | collective-permute-start | bytes 786440 | tf_op jit(solution)/shard_map/ppermute | solution.py:200
  25.1 10.5 %all_gather.7 = bf16[2,4,64,256]{3,2,0,1:T(8,128)(2,1)S(1)} all-gather(bf16[2,1,64,256]{3,2,0,1:T(8,128)(2,1)S(1)} %bitcast.165), channel_id=1, replica_groups=mesh['dy'=8,'dx'=4,'section'=4,'space'=4] {'space'}, dimensions={1}, use_global_device_ids=true | all-gather | bytes 327680 | tf_op jit(solution)/shard_map/all_gather | solution.py:176
  36.5 0.9 convolution_select_fusion.3
  40.4 0.9 convolution_select_fusion.5
  41.8 0.9 collective-permute-start.1
  45.2 0.8 convolution_select_fusion.4
  46.6 0.7 collective-permute-start.2
  48.6 1.8 multiply_reduce_fusion
  51.3 0.7 collective-permute-start.4
  52.0 1.3 collective-permute-start.7
  53.3 0.7 select_select_fusion
  55.7 0.9 convolution_select_fusion.2
  56.9 0.7 multiply_reduce_fusion.1
  58.6 0.9 collective-permute-start.5
  60.7 0.9 convolution_select_fusion.1
  62.0 0.7 multiply_reduce_fusion.2
  63.7 1.3 collective-permute-start.6
  65.3 1.6 copy.82
  67.0 2.4 %collective-permute-done.7 = bf16[2,4,64,256]{3,1,2,0:T(4,128)(2,1)S(1)} collective-permute-done((bf16[2,4,64,256]{3,1,2,0:T(4,128)(2,1)S(1)}, bf16[2,4,64,256]{3,1,2,0:T(4,128)(2,1)S(1)}, u32[]{:S(2)}, u32[]{:S(2)}) %collective-permute-start.7) | collective-permute-done | bytes 262176 | tf_op jit(solution)/shard_map/ppermute | solution.py:220
  69.4 19.1 %collective-permute-done.6 = bf16[2,4,64,256]{3,1,2,0:T(4,128)(2,1)S(1)} collective-permute-done((bf16[2,4,64,256]{3,1,2,0:T(4,128)(2,1)S(1)}, bf16[2,4,64,256]{3,1,2,0:T(4,128)(2,1)S(1)}, u32[]{:S(2)}, u32[]{:S(2)}) %collective-permute-start.6) | collective-permute-done | bytes 262176 | tf_op jit(solution)/shard_map/ppermute | solution.py:211
  90.0 0.9 convolution_select_fusion
  92.2 1.8 fusion.55
  94.3 3.1 %collective-permute-start.8 = (f32[368,256]{1,0:T(8,128)S(1)}, f32[368,256]{1,0:T(8,128)S(1)}, u32[]{:S(2)}, u32[]{:S(2)}) collective-permute-start(f32[368,256]{1,0:T(8,128)S(1)} %constant_dynamic-slice_fusion.2), channel_id=1, source_target_pairs={{0,16},{16,0},{32,48},{48,32},{1,17},{17,1},{33,49},{49,33},{2,18}... | collective-permute-start | bytes 1130504 | tf_op jit(solution)/shard_map/ppermute | solution.py:252
  97.4 5.2 %collective-permute-done.8 = f32[368,256]{1,0:T(8,128)S(1)} collective-permute-done((f32[368,256]{1,0:T(8,128)S(1)}, f32[368,256]{1,0:T(8,128)S(1)}, u32[]{:S(2)}, u32[]{:S(2)}) %collective-permute-start.8) | collective-permute-done | bytes 376864 | tf_op jit(solution)/shard_map/ppermute | solution.py:252
  102.7 4.7 %collective-permute-start.9 = (f32[184,256]{1,0:T(8,128)S(1)}, f32[184,256]{1,0:T(8,128)S(1)}, u32[]{:S(2)}, u32[]{:S(2)}) collective-permute-start(f32[184,256]{1,0:T(8,128)S(1)} %constant_dynamic-slice_fusion.1), channel_id=1, source_target_pairs={{0,32},{16,48},{32,0},{48,16},{1,33},{17,49},{33,1},{49,17},{2,34}... | collective-permute-start | bytes 565256 | tf_op jit(solution)/shard_map/ppermute | solution.py:252
  107.4 3.9 %collective-permute-done.9 = f32[184,256]{1,0:T(8,128)S(1)} collective-permute-done((f32[184,256]{1,0:T(8,128)S(1)}, f32[184,256]{1,0:T(8,128)S(1)}, u32[]{:S(2)}, u32[]{:S(2)}) %collective-permute-start.9) | collective-permute-done | bytes 188448 | tf_op jit(solution)/shard_map/ppermute | solution.py:252
  111.3 2.1 %collective-permute-start.10 = (f32[184,256]{1,0:T(8,128)S(1)}, f32[184,256]{1,0:T(8,128)S(1)}, u32[]{:S(2)}, u32[]{:S(2)}) collective-permute-start(f32[184,256]{1,0:T(8,128)S(1)} %dynamic-slice_add_fusion.1), channel_id=1, source_target_pairs={{0,64},{64,0},{128,192},{192,128},{256,320},{320,256},{384,448},{4... | collective-permute-start | bytes 565256 | tf_op jit(solution)/shard_map/ppermute | solution.py:261
  113.3 4.3 %collective-permute-done.10 = f32[184,256]{1,0:T(8,128)S(1)} collective-permute-done((f32[184,256]{1,0:T(8,128)S(1)}, f32[184,256]{1,0:T(8,128)S(1)}, u32[]{:S(2)}, u32[]{:S(2)}) %collective-permute-start.10) | collective-permute-done | bytes 188448 | tf_op jit(solution)/shard_map/ppermute | solution.py:261
  117.6 2.0 %collective-permute-start.11 = (f32[184,256]{1,0:T(8,128)S(1)}, f32[184,256]{1,0:T(8,128)S(1)}, u32[]{:S(2)}, u32[]{:S(2)}) collective-permute-start(f32[184,256]{1,0:T(8,128)S(1)} %add.291), channel_id=1, source_target_pairs={{0,128},{64,192},{128,0},{192,64},{256,384},{320,448},{384,256},{4... | collective-permute-start | bytes 565256 | tf_op jit(solution)/shard_map/ppermute | solution.py:261
  119.6 7.2 %collective-permute-done.11 = f32[184,256]{1,0:T(8,128)S(1)} collective-permute-done((f32[184,256]{1,0:T(8,128)S(1)}, f32[184,256]{1,0:T(8,128)S(1)}, u32[]{:S(2)}, u32[]{:S(2)}) %collective-permute-start.11) | collective-permute-done | bytes 188448 | tf_op jit(solution)/shard_map/ppermute | solution.py:261
  126.9 4.0 %collective-permute-start.12 = (f32[184,256]{1,0:T(8,128)S(1)}, f32[184,256]{1,0:T(8,128)S(1)}, u32[]{:S(2)}, u32[]{:S(2)}) collective-permute-start(f32[184,256]{1,0:T(8,128)S(1)} %add.292), channel_id=1, source_target_pairs={{0,256},{64,320},{128,384},{192,448},{256,0},{320,64},{384,128},{4... | collective-permute-start | bytes 565256 | tf_op jit(solution)/shard_map/ppermute | solution.py:261
  130.9 7.6 %collective-permute-done.12 = f32[184,256]{1,0:T(8,128)S(1)} collective-permute-done((f32[184,256]{1,0:T(8,128)S(1)}, f32[184,256]{1,0:T(8,128)S(1)}, u32[]{:S(2)}, u32[]{:S(2)}) %collective-permute-start.12) | collective-permute-done | bytes 188448 | tf_op jit(solution)/shard_map/ppermute | solution.py:261
  138.5 6.4 %collective-permute-start.13 = (bf16[184,256]{1,0:T(8,128)(2,1)S(1)}, bf16[184,256]{1,0:T(8,128)(2,1)S(1)}, u32[]{:S(2)}, u32[]{:S(2)}) collective-permute-start(bf16[184,256]{1,0:T(8,128)(2,1)S(1)} %add_convert_fusion.2), channel_id=1, source_target_pairs={{0,32},{16,48},{32,0},{48,16},{1,33},{17,49},{33,1},{49,17},{2,34}... | collective-permute-start | bytes 282632 | tf_op jit(solution)/shard_map/ppermute | solution.py:271
  145.0 1.9 %collective-permute-done.13 = bf16[184,256]{1,0:T(8,128)(2,1)S(1)} collective-permute-done((bf16[184,256]{1,0:T(8,128)(2,1)S(1)}, bf16[184,256]{1,0:T(8,128)(2,1)S(1)}, u32[]{:S(2)}, u32[]{:S(2)}) %collective-permute-start.13) | collective-permute-done | bytes 94240 | tf_op jit(solution)/shard_map/ppermute | solution.py:271
  146.9 3.3 %collective-permute-start.14 = (bf16[368,256]{1,0:T(8,128)(2,1)S(1)}, bf16[368,256]{1,0:T(8,128)(2,1)S(1)}, u32[]{:S(2)}, u32[]{:S(2)}) collective-permute-start(bf16[368,256]{1,0:T(8,128)(2,1)S(1)} %constant_dynamic-update-slice_fusion.3), channel_id=1, source_target_pairs={{0,16},{16,0},{32,48},{48,32},{1,17},{17,1},{33,49},{49,33},{2,18}... | collective-permute-start | bytes 565256 | tf_op jit(solution)/shard_map/ppermute | solution.py:271
  150.3 2.9 %collective-permute-done.14 = bf16[368,256]{1,0:T(8,128)(2,1)S(1)} collective-permute-done((bf16[368,256]{1,0:T(8,128)(2,1)S(1)}, bf16[368,256]{1,0:T(8,128)(2,1)S(1)}, u32[]{:S(2)}, u32[]{:S(2)}) %collective-permute-start.14) | collective-permute-done | bytes 188448 | tf_op jit(solution)/shard_map/ppermute | solution.py:271
  153.2 10.6 %collective-permute-start.15 = (bf16[736,256]{1,0:T(8,128)(2,1)S(1)}, bf16[736,256]{1,0:T(8,128)(2,1)S(1)}, u32[]{:S(2)}, u32[]{:S(2)}) collective-permute-start(bf16[736,256]{1,0:T(8,128)(2,1)S(1)} %constant_dynamic-update-slice_fusion.2), channel_id=1, source_target_pairs={{0,2},{1,3},{2,0},{3,1},{4,6},{5,7},{6,4},{7,5},{8,10},{9,11},{10,... | collective-permute-start | bytes 1130504 | tf_op jit(solution)/shard_map/ppermute | solution.py:271
  163.9 4.9 %collective-permute-done.15 = bf16[736,256]{1,0:T(8,128)(2,1)S(1)} collective-permute-done((bf16[736,256]{1,0:T(8,128)(2,1)S(1)}, bf16[736,256]{1,0:T(8,128)(2,1)S(1)}, u32[]{:S(2)}, u32[]{:S(2)}) %collective-permute-start.15) | collective-permute-done | bytes 376864 | tf_op jit(solution)/shard_map/ppermute | solution.py:271
  168.9 18.2 %collective-permute-start.16 = (bf16[1472,256]{1,0:T(8,128)(2,1)S(1)}, bf16[1472,256]{1,0:T(8,128)(2,1)S(1)}, u32[]{:S(2)}, u32[]{:S(2)}) collective-permute-start(bf16[1472,256]{1,0:T(8,128)(2,1)S(1)} %constant_dynamic-update-slice_fusion.1), channel_id=1, source_target_pairs={{0,1},{1,0},{2,3},{3,2},{4,5},{5,4},{6,7},{7,6},{8,9},{9,8},{10,11... | collective-permute-start | bytes 2261000 | tf_op jit(solution)/shard_map/ppermute | solution.py:271
  187.2 1.7 collective-permute-done.16
  189.2 1.6 slice.95
  191.4 0.9 reshape.165
  (121 shorter events, 21.9 us)
Async XLA Ops:
  0.6 12.3 %copy-start = (bf16[1,3,3,256,256]{4,3,2,1,0:T(8,128)(2,1)S(1)}, bf16[1,3,3,256,256]{4,3,2,1,0:T(8,128)(2,1)}, u32[]{:S(2)}) copy-start(bf16[1,3,3,256,256]{4,3,2,1,0:T(8,128)(2,1)} %param.9) | copy-start | bytes 3538948
  0.6 12.3 %copy-start.3 = (pred[16,9]{0,1:T(8,128)(4,1)S(1)}, pred[16,9]{0,1:T(8,128)(4,1)}, u32[]{:S(2)}) copy-start(pred[16,9]{0,1:T(8,128)(4,1)} %constant.217) | copy-start | bytes 436
  13.0 12.1 %copy-start.2 = (bf16[2,1,64,256]{3,2,1,0:T(8,128)(2,1)S(1)}, bf16[2,1,64,256]{3,2,1,0:T(8,128)(2,1)}, u32[]{:S(2)}) copy-start(bf16[2,1,64,256]{3,2,1,0:T(8,128)(2,1)} %param.8) | copy-start | bytes 196612
  14.5 23.8 %collective-permute-start = (bf16[2,4,64,256]{3,1,2,0:T(4,128)(2,1)S(1)}, bf16[2,4,64,256]{3,1,2,0:T(4,128)(2,1)S(1)}, u32[]{:S(2)}, u32[]{:S(2)}) collective-permute-start(bf16[2,4,64,256]{3,1,2,0:T(4,128)(2,1)S(1)} %fusion.79), channel_id=1, source_target_pairs={{0,4},{1,5},{2,6},{3,7},{16,20},{17,21},{18,22},{19,23},{32,36},{3... | collective-permute-start | bytes 786440 | tf_op jit(solution)/shard_map/ppermute | solution.py:195
  20.3 27.4 %collective-permute-start.3 = (bf16[2,4,64,256]{3,1,2,0:T(4,128)(2,1)S(1)}, bf16[2,4,64,256]{3,1,2,0:T(4,128)(2,1)S(1)}, u32[]{:S(2)}, u32[]{:S(2)}) collective-permute-start(bf16[2,4,64,256]{3,1,2,0:T(4,128)(2,1)S(1)} %fusion.79), channel_id=1, source_target_pairs={{0,12},{1,13},{2,14},{3,15},{16,28},{17,29},{18,30},{19,31},{32,44... | collective-permute-start | bytes 786440 | tf_op jit(solution)/shard_map/ppermute | solution.py:200
  36.1 1.8 copy-start.1
  41.8 1.3 collective-permute-start.1
  46.6 1.1 collective-permute-start.2
  51.3 3.4 %collective-permute-start.4 = (bf16[2,4,64,256]{3,1,2,0:T(4,128)(2,1)S(1)}, bf16[2,4,64,256]{3,1,2,0:T(4,128)(2,1)S(1)}, u32[]{:S(2)}, u32[]{:S(2)}) collective-permute-start(bf16[2,4,64,256]{3,1,2,0:T(4,128)(2,1)S(1)} %fusion.94), channel_id=1, source_target_pairs={{12,8},{13,9},{14,10},{15,11},{28,24},{29,25},{30,26},{31,27},{44,... | collective-permute-start | bytes 786440 | tf_op jit(solution)/shard_map/ppermute | solution.py:211
  52.0 17.4 %collective-permute-start.7 = (bf16[2,4,64,256]{3,1,2,0:T(4,128)(2,1)S(1)}, bf16[2,4,64,256]{3,1,2,0:T(4,128)(2,1)S(1)}, u32[]{:S(2)}, u32[]{:S(2)}) collective-permute-start(bf16[2,4,64,256]{3,1,2,0:T(4,128)(2,1)S(1)} %fusion.94), channel_id=1, source_target_pairs={{12,0},{13,1},{14,2},{15,3},{28,16},{29,17},{30,18},{31,19},{44,32... | collective-permute-start | bytes 786440 | tf_op jit(solution)/shard_map/ppermute | solution.py:220
  58.6 1.3 collective-permute-start.5
  63.7 24.8 %collective-permute-start.6 = (bf16[2,4,64,256]{3,1,2,0:T(4,128)(2,1)S(1)}, bf16[2,4,64,256]{3,1,2,0:T(4,128)(2,1)S(1)}, u32[]{:S(2)}, u32[]{:S(2)}) collective-permute-start(bf16[2,4,64,256]{3,1,2,0:T(4,128)(2,1)S(1)} %fusion.100), channel_id=1, source_target_pairs={{4,0},{5,1},{6,2},{7,3},{20,16},{21,17},{22,18},{23,19},{36,32},{3... | collective-permute-start | bytes 786440 | tf_op jit(solution)/shard_map/ppermute | solution.py:211
  94.3 8.3 %collective-permute-start.8 = (f32[368,256]{1,0:T(8,128)S(1)}, f32[368,256]{1,0:T(8,128)S(1)}, u32[]{:S(2)}, u32[]{:S(2)}) collective-permute-start(f32[368,256]{1,0:T(8,128)S(1)} %constant_dynamic-slice_fusion.2), channel_id=1, source_target_pairs={{0,16},{16,0},{32,48},{48,32},{1,17},{17,1},{33,49},{49,33},{2,18}... | collective-permute-start | bytes 1130504 | tf_op jit(solution)/shard_map/ppermute | solution.py:252
  102.7 8.5 %collective-permute-start.9 = (f32[184,256]{1,0:T(8,128)S(1)}, f32[184,256]{1,0:T(8,128)S(1)}, u32[]{:S(2)}, u32[]{:S(2)}) collective-permute-start(f32[184,256]{1,0:T(8,128)S(1)} %constant_dynamic-slice_fusion.1), channel_id=1, source_target_pairs={{0,32},{16,48},{32,0},{48,16},{1,33},{17,49},{33,1},{49,17},{2,34}... | collective-permute-start | bytes 565256 | tf_op jit(solution)/shard_map/ppermute | solution.py:252
  111.3 6.3 %collective-permute-start.10 = (f32[184,256]{1,0:T(8,128)S(1)}, f32[184,256]{1,0:T(8,128)S(1)}, u32[]{:S(2)}, u32[]{:S(2)}) collective-permute-start(f32[184,256]{1,0:T(8,128)S(1)} %dynamic-slice_add_fusion.1), channel_id=1, source_target_pairs={{0,64},{64,0},{128,192},{192,128},{256,320},{320,256},{384,448},{4... | collective-permute-start | bytes 565256 | tf_op jit(solution)/shard_map/ppermute | solution.py:261
  117.6 9.2 %collective-permute-start.11 = (f32[184,256]{1,0:T(8,128)S(1)}, f32[184,256]{1,0:T(8,128)S(1)}, u32[]{:S(2)}, u32[]{:S(2)}) collective-permute-start(f32[184,256]{1,0:T(8,128)S(1)} %add.291), channel_id=1, source_target_pairs={{0,128},{64,192},{128,0},{192,64},{256,384},{320,448},{384,256},{4... | collective-permute-start | bytes 565256 | tf_op jit(solution)/shard_map/ppermute | solution.py:261
  126.9 11.6 %collective-permute-start.12 = (f32[184,256]{1,0:T(8,128)S(1)}, f32[184,256]{1,0:T(8,128)S(1)}, u32[]{:S(2)}, u32[]{:S(2)}) collective-permute-start(f32[184,256]{1,0:T(8,128)S(1)} %add.292), channel_id=1, source_target_pairs={{0,256},{64,320},{128,384},{192,448},{256,0},{320,64},{384,128},{4... | collective-permute-start | bytes 565256 | tf_op jit(solution)/shard_map/ppermute | solution.py:261
  138.5 8.4 %collective-permute-start.13 = (bf16[184,256]{1,0:T(8,128)(2,1)S(1)}, bf16[184,256]{1,0:T(8,128)(2,1)S(1)}, u32[]{:S(2)}, u32[]{:S(2)}) collective-permute-start(bf16[184,256]{1,0:T(8,128)(2,1)S(1)} %add_convert_fusion.2), channel_id=1, source_target_pairs={{0,32},{16,48},{32,0},{48,16},{1,33},{17,49},{33,1},{49,17},{2,34}... | collective-permute-start | bytes 282632 | tf_op jit(solution)/shard_map/ppermute | solution.py:271
  146.9 6.3 %collective-permute-start.14 = (bf16[368,256]{1,0:T(8,128)(2,1)S(1)}, bf16[368,256]{1,0:T(8,128)(2,1)S(1)}, u32[]{:S(2)}, u32[]{:S(2)}) collective-permute-start(bf16[368,256]{1,0:T(8,128)(2,1)S(1)} %constant_dynamic-update-slice_fusion.3), channel_id=1, source_target_pairs={{0,16},{16,0},{32,48},{48,32},{1,17},{17,1},{33,49},{49,33},{2,18}... | collective-permute-start | bytes 565256 | tf_op jit(solution)/shard_map/ppermute | solution.py:271
  153.2 15.6 %collective-permute-start.15 = (bf16[736,256]{1,0:T(8,128)(2,1)S(1)}, bf16[736,256]{1,0:T(8,128)(2,1)S(1)}, u32[]{:S(2)}, u32[]{:S(2)}) collective-permute-start(bf16[736,256]{1,0:T(8,128)(2,1)S(1)} %constant_dynamic-update-slice_fusion.2), channel_id=1, source_target_pairs={{0,2},{1,3},{2,0},{3,1},{4,6},{5,7},{6,4},{7,5},{8,10},{9,11},{10,... | collective-permute-start | bytes 1130504 | tf_op jit(solution)/shard_map/ppermute | solution.py:271
  168.9 20.0 %collective-permute-start.16 = (bf16[1472,256]{1,0:T(8,128)(2,1)S(1)}, bf16[1472,256]{1,0:T(8,128)(2,1)S(1)}, u32[]{:S(2)}, u32[]{:S(2)}) collective-permute-start(bf16[1472,256]{1,0:T(8,128)(2,1)S(1)} %constant_dynamic-update-slice_fusion.1), channel_id=1, source_target_pairs={{0,1},{1,0},{2,3},{3,2},{4,5},{5,4},{6,7},{7,6},{8,9},{9,8},{10,11... | collective-permute-start | bytes 2261000 | tf_op jit(solution)/shard_map/ppermute | solution.py:271
where the time goes:
time: 193 us; the launch traced here: 192 us
  starting transfers between devices  70.6 us (37%)
  waiting for transfers between devices  61 us (32%)
  blocking collectives  18 us (9%)
  other arithmetic  15 us (8%)
  local copies, waits for them, and re-layouts  13 us (7%)
  matrix products  12.9 us (7%)
    ppermute x4, starting transfers between devices, butterfly_gather(): got = lax.ppermute(flat, axis, [(j, j ^ step) for j in range(count)])  38.6 us
    ppermute x3, waiting for transfers between devices, per_device(): upstream = lax.ppermute(carried, 'section', [(active + 1, active)])  19.1 us
    ppermute x3, waiting for transfers between devices, butterfly_sum(): lax.ppermute(flat, axis, [(j, j ^ step) for j in range(count)])  19 us
    ppermute x4, waiting for transfers between devices, butterfly_gather(): got = lax.ppermute(flat, axis, [(j, j ^ step) for j in range(count)])  11.4 us
    all_gather x1, blocking collectives, per_device(): out_grad = lax.all_gather(out_grad, 'space', axis=1, tiled=True)  10.5 us
    ppermute x2, waiting for transfers between devices, butterfly_scatter(): lax.ppermute(sent, axis, [(j, j ^ step) for j in range(count)])  9.03 us
    ppermute x3, starting transfers between devices, butterfly_sum(): lax.ppermute(flat, axis, [(j, j ^ step) for j in range(count)])  8.07 us
    ppermute x2, starting transfers between devices, butterfly_scatter(): lax.ppermute(sent, axis, [(j, j ^ step) for j in range(count)])  7.79 us
  transfers between devices with their start and end apart: 17, of which 11 were waited for; matrix products, arithmetic and copies ran while one was open for 11% of the time, Pallas kernels for 0%

commit v1 on v0

--- a/solution.py
+++ b/solution.py
@@ -173,7 +173,9 @@
     section_count = lax.axis_size("section")
     section_no = lax.axis_index("section")
     images = lax.all_gather(images, "space", axis=1, tiled=True)
-    out_grad = lax.all_gather(out_grad, "space", axis=1, tiled=True)
+    out_grad = jnp.concatenate(
+        lax.all_to_all(jnp.stack([out_grad] * lax.axis_size("space")), "space", 0, 0), axis=1
+    )
     row_count = images.shape[1]
     col_count = images.shape[2]
     channels = images.shape[3]

time: 193 us -> 190 us (0.984)
  the two profiles are of different devices: /device:TPU:25 before, /device:TPU:7 now
where the time goes in v1:
time: 190 us
  starting transfers between devices  79.1 us (42%)
  waiting for transfers between devices  57.6 us (30%)
  other arithmetic  15 us (8%)
  matrix products  14.8 us (8%)
  local copies, waits for them, and re-layouts  14 us (7%)
  blocking collectives  7.48 us (4%)
    ppermute x4, starting transfers between devices, butterfly_gather(): got = lax.ppermute(flat, axis, [(j, j ^ step) for j in range(count)])  38.7 us
    ppermute x3, waiting for transfers between devices, per_device(): upstream = lax.ppermute(carried, 'section', [(active + 1, active)])  19.1 us
    ppermute x3, starting transfers between devices, butterfly_sum(): lax.ppermute(flat, axis, [(j, j ^ step) for j in range(count)])  14.5 us
    ppermute x4, waiting for transfers between devices, butterfly_gather(): got = lax.ppermute(flat, axis, [(j, j ^ step) for j in range(count)])  12.6 us
    ppermute x3, waiting for transfers between devices, butterfly_sum(): lax.ppermute(flat, axis, [(j, j ^ step) for j in range(count)])  12.1 us
    ppermute x2, waiting for transfers between devices, butterfly_scatter(): lax.ppermute(sent, axis, [(j, j ^ step) for j in range(count)])  10.5 us
    all_gather x1, blocking collectives, per_device(): images = lax.all_gather(images, 'space', axis=1, tiled=True)  7.48 us
    ppermute x3, starting transfers between devices, per_device(): inputs = lax.ppermute(carried, 'section', [(moment - 1, moment)])  7.36 us
  transfers between devices with their start and end apart: 18, of which 11 were waited for; matrix products, arithmetic and copies ran while one was open for 13% of the time, Pallas kernels for 0%

profile of v1, /device:TPU:7, one launch (start us, length us, event | category | flops | bytes accessed | tf_op | source)
XLA Modules:
  0.0 189.8 jit_solution(8575595817062132129)
XLA Ops:
  0.7 7.5 %all_gather.3 = bf16[2,4,64,256]{3,2,0,1:T(8,128)(2,1)S(1)} all-gather(bf16[2,1,64,256]{3,2,0,1:T(8,128)(2,1)} %bitcast.176), channel_id=1, replica_groups=mesh['dy'=8,'dx'=4,'section'=4,'space'=4] {'space'}, dimensions={1}, use_global_device_ids=true | all-gather | bytes 327680 | tf_op jit(solution)/shard_map/all_gather | solution.py:175
  9.2 1.2 fusion.132
  10.6 0.9 broadcast_multiply_fusion.3
  11.5 1.2 fusion.223
  13.6 0.9 convolution_select_fusion.6
  15.1 5.8 %collective-permute-start = (bf16[2,4,64,256]{3,1,2,0:T(4,128)(2,1)S(1)}, bf16[2,4,64,256]{3,1,2,0:T(4,128)(2,1)S(1)}, u32[]{:S(2)}, u32[]{:S(2)}) collective-permute-start(bf16[2,4,64,256]{3,1,2,0:T(4,128)(2,1)S(1)} %fusion.79), channel_id=1, source_target_pairs={{0,4},{1,5},{2,6},{3,7},{16,20},{17,21},{18,22},{19,23},{32,36},{3... | collective-permute-start | bytes 786440 | tf_op jit(solution)/shard_map/ppermute | solution.py:197
  21.0 4.7 %collective-permute-start.3 = (bf16[2,4,64,256]{3,1,2,0:T(4,128)(2,1)S(1)}, bf16[2,4,64,256]{3,1,2,0:T(4,128)(2,1)S(1)}, u32[]{:S(2)}, u32[]{:S(2)}) collective-permute-start(bf16[2,4,64,256]{3,1,2,0:T(4,128)(2,1)S(1)} %fusion.79), channel_id=1, source_target_pairs={{0,12},{1,13},{2,14},{3,15},{16,28},{17,29},{18,30},{19,31},{32,44... | collective-permute-start | bytes 786440 | tf_op jit(solution)/shard_map/ppermute | solution.py:202
  25.7 0.7 stack.2
  26.4 3.8 %all-to-all-start = ((bf16[4,2,1,64,256]{4,3,1,2,0:T(8,128)(2,1)}), bf16[4,2,1,64,256]{4,3,1,2,0:T(8,128)(2,1)S(1)}, u32[]{:S(2)}, u32[]{:S(2)}) async-start(bf16[4,2,1,64,256]{4,3,1,2,0:T(8,128)(2,1)} %stack.2), calls=%async_computation | async-start | bytes 524288 | tf_op jit(solution)/shard_map/all_to_all | solution.py:177
  31.2 0.9 broadcast_multiply_fusion.2
  33.4 0.9 convolution_select_fusion.5
  34.8 0.9 collective-permute-start.1
  37.3 1.6 convolution_select_fusion.3
  41.3 0.9 convolution_select_fusion.4
  42.8 0.7 collective-permute-start.2
  44.8 1.8 multiply_reduce_fusion
  48.2 1.5 collective-permute-start.7
  52.1 0.9 convolution_select_fusion.2
  53.4 0.7 multiply_reduce_fusion.1
  55.0 0.7 collective-permute-start.5
  56.9 0.9 convolution_select_fusion.1
  58.2 0.7 multiply_reduce_fusion.2
  59.9 1.6 collective-permute-start.6
  61.8 1.6 copy.80
  63.4 3.3 %collective-permute-done.7 = bf16[2,4,64,256]{3,1,2,0:T(4,128)(2,1)S(1)} collective-permute-done((bf16[2,4,64,256]{3,1,2,0:T(4,128)(2,1)S(1)}, bf16[2,4,64,256]{3,1,2,0:T(4,128)(2,1)S(1)}, u32[]{:S(2)}, u32[]{:S(2)}) %collective-permute-start.7) | collective-permute-done | bytes 262176 | tf_op jit(solution)/shard_map/ppermute | solution.py:222
  66.7 19.1 %collective-permute-done.6 = bf16[2,4,64,256]{3,1,2,0:T(4,128)(2,1)S(1)} collective-permute-done((bf16[2,4,64,256]{3,1,2,0:T(4,128)(2,1)S(1)}, bf16[2,4,64,256]{3,1,2,0:T(4,128)(2,1)S(1)}, u32[]{:S(2)}, u32[]{:S(2)}) %collective-permute-start.6) | collective-permute-done | bytes 262176 | tf_op jit(solution)/shard_map/ppermute | solution.py:213
  87.4 0.9 convolution_select_fusion
  89.6 1.8 fusion.55
  91.6 2.5 %collective-permute-start.8 = (f32[368,256]{1,0:T(8,128)S(1)}, f32[368,256]{1,0:T(8,128)S(1)}, u32[]{:S(2)}, u32[]{:S(2)}) collective-permute-start(f32[368,256]{1,0:T(8,128)S(1)} %constant_dynamic-slice_fusion.2), channel_id=1, source_target_pairs={{0,16},{16,0},{32,48},{48,32},{1,17},{17,1},{33,49},{49,33},{2,18}... | collective-permute-start | bytes 1130504 | tf_op jit(solution)/shard_map/ppermute | solution.py:254
  94.2 5.8 %collective-permute-done.8 = f32[368,256]{1,0:T(8,128)S(1)} collective-permute-done((f32[368,256]{1,0:T(8,128)S(1)}, f32[368,256]{1,0:T(8,128)S(1)}, u32[]{:S(2)}, u32[]{:S(2)}) %collective-permute-start.8) | collective-permute-done | bytes 376864 | tf_op jit(solution)/shard_map/ppermute | solution.py:254
  100.1 3.1 %collective-permute-start.9 = (f32[184,256]{1,0:T(8,128)S(1)}, f32[184,256]{1,0:T(8,128)S(1)}, u32[]{:S(2)}, u32[]{:S(2)}) collective-permute-start(f32[184,256]{1,0:T(8,128)S(1)} %constant_dynamic-slice_fusion.1), channel_id=1, source_target_pairs={{0,32},{16,48},{32,0},{48,16},{1,33},{17,49},{33,1},{49,17},{2,34}... | collective-permute-start | bytes 565256 | tf_op jit(solution)/shard_map/ppermute | solution.py:254
  103.2 4.7 %collective-permute-done.9 = f32[184,256]{1,0:T(8,128)S(1)} collective-permute-done((f32[184,256]{1,0:T(8,128)S(1)}, f32[184,256]{1,0:T(8,128)S(1)}, u32[]{:S(2)}, u32[]{:S(2)}) %collective-permute-start.9) | collective-permute-done | bytes 188448 | tf_op jit(solution)/shard_map/ppermute | solution.py:254
  107.9 3.3 %collective-permute-start.10 = (f32[184,256]{1,0:T(8,128)S(1)}, f32[184,256]{1,0:T(8,128)S(1)}, u32[]{:S(2)}, u32[]{:S(2)}) collective-permute-start(f32[184,256]{1,0:T(8,128)S(1)} %dynamic-slice_add_fusion.1), channel_id=1, source_target_pairs={{0,64},{64,0},{128,192},{192,128},{256,320},{320,256},{384,448},{4... | collective-permute-start | bytes 565256 | tf_op jit(solution)/shard_map/ppermute | solution.py:263
  111.2 3.3 %collective-permute-done.10 = f32[184,256]{1,0:T(8,128)S(1)} collective-permute-done((f32[184,256]{1,0:T(8,128)S(1)}, f32[184,256]{1,0:T(8,128)S(1)}, u32[]{:S(2)}, u32[]{:S(2)}) %collective-permute-start.10) | collective-permute-done | bytes 188448 | tf_op jit(solution)/shard_map/ppermute | solution.py:263
  114.6 4.1 %collective-permute-start.11 = (f32[184,256]{1,0:T(8,128)S(1)}, f32[184,256]{1,0:T(8,128)S(1)}, u32[]{:S(2)}, u32[]{:S(2)}) collective-permute-start(f32[184,256]{1,0:T(8,128)S(1)} %add.291), channel_id=1, source_target_pairs={{0,128},{64,192},{128,0},{192,64},{256,384},{320,448},{384,256},{4... | collective-permute-start | bytes 565256 | tf_op jit(solution)/shard_map/ppermute | solution.py:263
  118.7 5.0 %collective-permute-done.11 = f32[184,256]{1,0:T(8,128)S(1)} collective-permute-done((f32[184,256]{1,0:T(8,128)S(1)}, f32[184,256]{1,0:T(8,128)S(1)}, u32[]{:S(2)}, u32[]{:S(2)}) %collective-permute-start.11) | collective-permute-done | bytes 188448 | tf_op jit(solution)/shard_map/ppermute | solution.py:263
  123.8 7.0 %collective-permute-start.12 = (f32[184,256]{1,0:T(8,128)S(1)}, f32[184,256]{1,0:T(8,128)S(1)}, u32[]{:S(2)}, u32[]{:S(2)}) collective-permute-start(f32[184,256]{1,0:T(8,128)S(1)} %add.292), channel_id=1, source_target_pairs={{0,256},{64,320},{128,384},{192,448},{256,0},{320,64},{384,128},{4... | collective-permute-start | bytes 565256 | tf_op jit(solution)/shard_map/ppermute | solution.py:263
  130.8 3.7 %collective-permute-done.12 = f32[184,256]{1,0:T(8,128)S(1)} collective-permute-done((f32[184,256]{1,0:T(8,128)S(1)}, f32[184,256]{1,0:T(8,128)S(1)}, u32[]{:S(2)}, u32[]{:S(2)}) %collective-permute-start.12) | collective-permute-done | bytes 188448 | tf_op jit(solution)/shard_map/ppermute | solution.py:263
  134.6 5.7 %collective-permute-start.13 = (bf16[184,256]{1,0:T(8,128)(2,1)S(1)}, bf16[184,256]{1,0:T(8,128)(2,1)S(1)}, u32[]{:S(2)}, u32[]{:S(2)}) collective-permute-start(bf16[184,256]{1,0:T(8,128)(2,1)S(1)} %add_convert_fusion.2), channel_id=1, source_target_pairs={{0,32},{16,48},{32,0},{48,16},{1,33},{17,49},{33,1},{49,17},{2,34}... | collective-permute-start | bytes 282632 | tf_op jit(solution)/shard_map/ppermute | solution.py:273
  140.3 1.9 %collective-permute-done.13 = bf16[184,256]{1,0:T(8,128)(2,1)S(1)} collective-permute-done((bf16[184,256]{1,0:T(8,128)(2,1)S(1)}, bf16[184,256]{1,0:T(8,128)(2,1)S(1)}, u32[]{:S(2)}, u32[]{:S(2)}) %collective-permute-start.13) | collective-permute-done | bytes 94240 | tf_op jit(solution)/shard_map/ppermute | solution.py:273
  142.2 2.4 %collective-permute-start.14 = (bf16[368,256]{1,0:T(8,128)(2,1)S(1)}, bf16[368,256]{1,0:T(8,128)(2,1)S(1)}, u32[]{:S(2)}, u32[]{:S(2)}) collective-permute-start(bf16[368,256]{1,0:T(8,128)(2,1)S(1)} %constant_dynamic-update-slice_fusion.3), channel_id=1, source_target_pairs={{0,16},{16,0},{32,48},{48,32},{1,17},{17,1},{33,49},{49,33},{2,18}... | collective-permute-start | bytes 565256 | tf_op jit(solution)/shard_map/ppermute | solution.py:273
  144.7 4.1 %collective-permute-done.14 = bf16[368,256]{1,0:T(8,128)(2,1)S(1)} collective-permute-done((bf16[368,256]{1,0:T(8,128)(2,1)S(1)}, bf16[368,256]{1,0:T(8,128)(2,1)S(1)}, u32[]{:S(2)}, u32[]{:S(2)}) %collective-permute-start.14) | collective-permute-done | bytes 188448 | tf_op jit(solution)/shard_map/ppermute | solution.py:273
  148.9 9.6 %collective-permute-start.15 = (bf16[736,256]{1,0:T(8,128)(2,1)S(1)}, bf16[736,256]{1,0:T(8,128)(2,1)S(1)}, u32[]{:S(2)}, u32[]{:S(2)}) collective-permute-start(bf16[736,256]{1,0:T(8,128)(2,1)S(1)} %constant_dynamic-update-slice_fusion.2), channel_id=1, source_target_pairs={{0,2},{1,3},{2,0},{3,1},{4,6},{5,7},{6,4},{7,5},{8,10},{9,11},{10,... | collective-permute-start | bytes 1130504 | tf_op jit(solution)/shard_map/ppermute | solution.py:273
  158.6 4.9 %collective-permute-done.15 = bf16[736,256]{1,0:T(8,128)(2,1)S(1)} collective-permute-done((bf16[736,256]{1,0:T(8,128)(2,1)S(1)}, bf16[736,256]{1,0:T(8,128)(2,1)S(1)}, u32[]{:S(2)}, u32[]{:S(2)}) %collective-permute-start.15) | collective-permute-done | bytes 376864 | tf_op jit(solution)/shard_map/ppermute | solution.py:273
  163.5 21.0 %collective-permute-start.16 = (bf16[1472,256]{1,0:T(8,128)(2,1)S(1)}, bf16[1472,256]{1,0:T(8,128)(2,1)S(1)}, u32[]{:S(2)}, u32[]{:S(2)}) collective-permute-start(bf16[1472,256]{1,0:T(8,128)(2,1)S(1)} %constant_dynamic-update-slice_fusion.1), channel_id=1, source_target_pairs={{0,1},{1,0},{2,3},{3,2},{4,5},{5,4},{6,7},{7,6},{8,9},{9,8},{10,11... | collective-permute-start | bytes 2261000 | tf_op jit(solution)/shard_map/ppermute | solution.py:273
  184.7 1.7 collective-permute-done.16
  186.7 1.6 slice.95
  188.9 0.9 reshape.176
  (150 shorter events, 23.6 us)
Async XLA Ops:
  0.6 12.9 %copy-start = (bf16[1,3,3,256,256]{4,3,2,1,0:T(8,128)(2,1)S(1)}, bf16[1,3,3,256,256]{4,3,2,1,0:T(8,128)(2,1)}, u32[]{:S(2)}) copy-start(bf16[1,3,3,256,256]{4,3,2,1,0:T(8,128)(2,1)} %param.9) | copy-start | bytes 3538948
  0.6 12.9 %copy-start.9 = (pred[16,9]{0,1:T(8,128)(4,1)S(1)}, pred[16,9]{0,1:T(8,128)(4,1)}, u32[]{:S(2)}) copy-start(pred[16,9]{0,1:T(8,128)(4,1)} %constant.217) | copy-start | bytes 436
  0.7 30.6 %copy-start.7 = (s32[256]{0:T(256)}, s32[256]{0:T(256)S(1)}, u32[]{:S(2)}) copy-start(s32[256]{0:T(256)S(1)} %and_select_fusion) | copy-start | bytes 3076
  9.2 4.0 %copy-start.3 = (f32[2,128]{1,0:T(2,128)}, f32[2,128]{1,0:T(2,128)S(1)}, u32[]{:S(2)}) copy-start(f32[2,128]{1,0:T(2,128)S(1)} %get-tuple-element.49) | copy-start | bytes 3076
  9.2 4.0 %copy-start.5 = (f32[2,128]{1,0:T(2,128)}, f32[2,128]{1,0:T(2,128)S(1)}, u32[]{:S(2)}) copy-start(f32[2,128]{1,0:T(2,128)S(1)} %get-tuple-element.50) | copy-start | bytes 3076
  10.6 3.8 %copy-start.11 = (f32[2,256]{1,0:T(2,128)}, f32[2,256]{1,0:T(2,128)S(1)}, u32[]{:S(2)}) copy-start(f32[2,256]{1,0:T(2,128)S(1)} %fusion.31) | copy-start | bytes 6148
  13.6 12.1 %copy-start.2 = (bf16[2,1,64,256]{3,2,1,0:T(8,128)(2,1)S(1)}, bf16[2,1,64,256]{3,2,1,0:T(8,128)(2,1)}, u32[]{:S(2)}) copy-start(bf16[2,1,64,256]{3,2,1,0:T(8,128)(2,1)} %param.8) | copy-start | bytes 196612
  14.5 15.8 %copy-start.1 = (f32[1,256]{1,0:T(1,128)S(1)}, f32[1,256]{1,0:T(1,128)}, u32[]{:S(2)}) copy-start(f32[1,256]{1,0:T(1,128)} %param.10) | copy-start | bytes 3076
  15.1 15.6 %collective-permute-start = (bf16[2,4,64,256]{3,1,2,0:T(4,128)(2,1)S(1)}, bf16[2,4,64,256]{3,1,2,0:T(4,128)(2,1)S(1)}, u32[]{:S(2)}, u32[]{:S(2)}) collective-permute-start(bf16[2,4,64,256]{3,1,2,0:T(4,128)(2,1)S(1)} %fusion.79), channel_id=1, source_target_pairs={{0,4},{1,5},{2,6},{3,7},{16,20},{17,21},{18,22},{19,23},{32,36},{3... | collective-permute-start | bytes 786440 | tf_op jit(solution)/shard_map/ppermute | solution.py:197
  21.0 22.9 %collective-permute-start.3 = (bf16[2,4,64,256]{3,1,2,0:T(4,128)(2,1)S(1)}, bf16[2,4,64,256]{3,1,2,0:T(4,128)(2,1)S(1)}, u32[]{:S(2)}, u32[]{:S(2)}) collective-permute-start(bf16[2,4,64,256]{3,1,2,0:T(4,128)(2,1)S(1)} %fusion.79), channel_id=1, source_target_pairs={{0,12},{1,13},{2,14},{3,15},{16,28},{17,29},{18,30},{19,31},{32,44... | collective-permute-start | bytes 786440 | tf_op jit(solution)/shard_map/ppermute | solution.py:202
  26.4 9.7 %all-to-all-start = ((bf16[4,2,1,64,256]{4,3,1,2,0:T(8,128)(2,1)}), bf16[4,2,1,64,256]{4,3,1,2,0:T(8,128)(2,1)S(1)}, u32[]{:S(2)}, u32[]{:S(2)}) async-start(bf16[4,2,1,64,256]{4,3,1,2,0:T(8,128)(2,1)} %stack.2), calls=%async_computation | async-start | bytes 524288 | tf_op jit(solution)/shard_map/all_to_all | solution.py:177
  31.2 3.1 %copy-start.13 = (f32[2,256]{1,0:T(2,128)}, f32[2,256]{1,0:T(2,128)S(1)}, u32[]{:S(2)}) copy-start(f32[2,256]{1,0:T(2,128)S(1)} %fusion.27) | copy-start | bytes 6148
  34.8 4.4 %collective-permute-start.1 = (bf16[2,4,64,256]{3,1,2,0:T(4,128)(2,1)S(1)}, bf16[2,4,64,256]{3,1,2,0:T(4,128)(2,1)S(1)}, u32[]{:S(2)}, u32[]{:S(2)}) collective-permute-start(bf16[2,4,64,256]{3,1,2,0:T(4,128)(2,1)S(1)} %fusion.85), channel_id=1, source_target_pairs={{4,8},{5,9},{6,10},{7,11},{20,24},{21,25},{22,26},{23,27},{36,40},... | collective-permute-start | bytes 786440 | tf_op jit(solution)/shard_map/ppermute | solution.py:197
  37.2 2.2 %copy-start.8 = (s32[256]{0:T(256)S(1)}, s32[256]{0:T(256)}, u32[]{:S(2)}) copy-start(s32[256]{0:T(256)} %copy-done.7) | copy-start | bytes 3076
  38.8 2.5 %copy-start.10 = (pred[16,9]{0,1:T(8,128)(4,1)S(1)}, pred[16,9]{0,1:T(8,128)(4,1)}, u32[]{:S(2)}) copy-start(pred[16,9]{0,1:T(8,128)(4,1)} %constant.217) | copy-start | bytes 436
  42.2 2.3 %copy-start.12 = (f32[2,256]{1,0:T(2,128)S(1)}, f32[2,256]{1,0:T(2,128)}, u32[]{:S(2)}) copy-start(f32[2,256]{1,0:T(2,128)} %copy-done.11) | copy-start | bytes 6148
  42.2 2.3 %copy-start.14 = (f32[2,256]{1,0:T(2,128)S(1)}, f32[2,256]{1,0:T(2,128)}, u32[]{:S(2)}) copy-start(f32[2,256]{1,0:T(2,128)} %copy-done.13) | copy-start | bytes 6148
  42.2 2.3 %copy-start.15 = (f32[2,256]{1,0:T(2,128)S(1)}, f32[2,256]{1,0:T(2,128)}, u32[]{:S(2)}) copy-start(f32[2,256]{1,0:T(2,128)} %get-tuple-element.51) | copy-start | bytes 6148
  42.2 2.3 %copy-start.16 = (f32[2,256]{1,0:T(2,128)S(1)}, f32[2,256]{1,0:T(2,128)}, u32[]{:S(2)}) copy-start(f32[2,256]{1,0:T(2,128)} %get-tuple-element.52) | copy-start | bytes 6148
  42.8 1.1 collective-permute-start.2
  47.5 3.7 %collective-permute-start.4 = (bf16[2,4,64,256]{3,1,2,0:T(4,128)(2,1)S(1)}, bf16[2,4,64,256]{3,1,2,0:T(4,128)(2,1)S(1)}, u32[]{:S(2)}, u32[]{:S(2)}) collective-permute-start(bf16[2,4,64,256]{3,1,2,0:T(4,128)(2,1)S(1)} %fusion.94), channel_id=1, source_target_pairs={{12,8},{13,9},{14,10},{15,11},{28,24},{29,25},{30,26},{31,27},{44,... | collective-permute-start | bytes 786440 | tf_op jit(solution)/shard_map/ppermute | solution.py:213
  48.2 18.5 %collective-permute-start.7 = (bf16[2,4,64,256]{3,1,2,0:T(4,128)(2,1)S(1)}, bf16[2,4,64,256]{3,1,2,0:T(4,128)(2,1)S(1)}, u32[]{:S(2)}, u32[]{:S(2)}) collective-permute-start(bf16[2,4,64,256]{3,1,2,0:T(4,128)(2,1)S(1)} %fusion.94), channel_id=1, source_target_pairs={{12,0},{13,1},{14,2},{15,3},{28,16},{29,17},{30,18},{31,19},{44,32... | collective-permute-start | bytes 786440 | tf_op jit(solution)/shard_map/ppermute | solution.py:222
  55.0 1.1 collective-permute-start.5
  59.9 26.0 %collective-permute-start.6 = (bf16[2,4,64,256]{3,1,2,0:T(4,128)(2,1)S(1)}, bf16[2,4,64,256]{3,1,2,0:T(4,128)(2,1)S(1)}, u32[]{:S(2)}, u32[]{:S(2)}) collective-permute-start(bf16[2,4,64,256]{3,1,2,0:T(4,128)(2,1)S(1)} %fusion.100), channel_id=1, source_target_pairs={{4,0},{5,1},{6,2},{7,3},{20,16},{21,17},{22,18},{23,19},{36,32},{3... | collective-permute-start | bytes 786440 | tf_op jit(solution)/shard_map/ppermute | solution.py:213
  87.3 1.8 copy-start.4
  87.3 1.8 copy-start.6
  91.6 8.3 %collective-permute-start.8 = (f32[368,256]{1,0:T(8,128)S(1)}, f32[368,256]{1,0:T(8,128)S(1)}, u32[]{:S(2)}, u32[]{:S(2)}) collective-permute-start(f32[368,256]{1,0:T(8,128)S(1)} %constant_dynamic-slice_fusion.2), channel_id=1, source_target_pairs={{0,16},{16,0},{32,48},{48,32},{1,17},{17,1},{33,49},{49,33},{2,18}... | collective-permute-start | bytes 1130504 | tf_op jit(solution)/shard_map/ppermute | solution.py:254
  100.1 7.8 %collective-permute-start.9 = (f32[184,256]{1,0:T(8,128)S(1)}, f32[184,256]{1,0:T(8,128)S(1)}, u32[]{:S(2)}, u32[]{:S(2)}) collective-permute-start(f32[184,256]{1,0:T(8,128)S(1)} %constant_dynamic-slice_fusion.1), channel_id=1, source_target_pairs={{0,32},{16,48},{32,0},{48,16},{1,33},{17,49},{33,1},{49,17},{2,34}... | collective-permute-start | bytes 565256 | tf_op jit(solution)/shard_map/ppermute | solution.py:254
  107.9 6.6 %collective-permute-start.10 = (f32[184,256]{1,0:T(8,128)S(1)}, f32[184,256]{1,0:T(8,128)S(1)}, u32[]{:S(2)}, u32[]{:S(2)}) collective-permute-start(f32[184,256]{1,0:T(8,128)S(1)} %dynamic-slice_add_fusion.1), channel_id=1, source_target_pairs={{0,64},{64,0},{128,192},{192,128},{256,320},{320,256},{384,448},{4... | collective-permute-start | bytes 565256 | tf_op jit(solution)/shard_map/ppermute | solution.py:263
  114.6 9.2 %collective-permute-start.11 = (f32[184,256]{1,0:T(8,128)S(1)}, f32[184,256]{1,0:T(8,128)S(1)}, u32[]{:S(2)}, u32[]{:S(2)}) collective-permute-start(f32[184,256]{1,0:T(8,128)S(1)} %add.291), channel_id=1, source_target_pairs={{0,128},{64,192},{128,0},{192,64},{256,384},{320,448},{384,256},{4... | collective-permute-start | bytes 565256 | tf_op jit(solution)/shard_map/ppermute | solution.py:263
  123.8 10.8 %collective-permute-start.12 = (f32[184,256]{1,0:T(8,128)S(1)}, f32[184,256]{1,0:T(8,128)S(1)}, u32[]{:S(2)}, u32[]{:S(2)}) collective-permute-start(f32[184,256]{1,0:T(8,128)S(1)} %add.292), channel_id=1, source_target_pairs={{0,256},{64,320},{128,384},{192,448},{256,0},{320,64},{384,128},{4... | collective-permute-start | bytes 565256 | tf_op jit(solution)/shard_map/ppermute | solution.py:263
  134.6 7.6 %collective-permute-start.13 = (bf16[184,256]{1,0:T(8,128)(2,1)S(1)}, bf16[184,256]{1,0:T(8,128)(2,1)S(1)}, u32[]{:S(2)}, u32[]{:S(2)}) collective-permute-start(bf16[184,256]{1,0:T(8,128)(2,1)S(1)} %add_convert_fusion.2), channel_id=1, source_target_pairs={{0,32},{16,48},{32,0},{48,16},{1,33},{17,49},{33,1},{49,17},{2,34}... | collective-permute-start | bytes 282632 | tf_op jit(solution)/shard_map/ppermute | solution.py:273
  142.2 6.6 %collective-permute-start.14 = (bf16[368,256]{1,0:T(8,128)(2,1)S(1)}, bf16[368,256]{1,0:T(8,128)(2,1)S(1)}, u32[]{:S(2)}, u32[]{:S(2)}) collective-permute-start(bf16[368,256]{1,0:T(8,128)(2,1)S(1)} %constant_dynamic-update-slice_fusion.3), channel_id=1, source_target_pairs={{0,16},{16,0},{32,48},{48,32},{1,17},{17,1},{33,49},{49,33},{2,18}... | collective-permute-start | bytes 565256 | tf_op jit(solution)/shard_map/ppermute | solution.py:273
  148.9 14.6 %collective-permute-start.15 = (bf16[736,256]{1,0:T(8,128)(2,1)S(1)}, bf16[736,256]{1,0:T(8,128)(2,1)S(1)}, u32[]{:S(2)}, u32[]{:S(2)}) collective-permute-start(bf16[736,256]{1,0:T(8,128)(2,1)S(1)} %constant_dynamic-update-slice_fusion.2), channel_id=1, source_target_pairs={{0,2},{1,3},{2,0},{3,1},{4,6},{5,7},{6,4},{7,5},{8,10},{9,11},{10,... | collective-permute-start | bytes 1130504 | tf_op jit(solution)/shard_map/ppermute | solution.py:273
  163.5 22.8 %collective-permute-start.16 = (bf16[1472,256]{1,0:T(8,128)(2,1)S(1)}, bf16[1472,256]{1,0:T(8,128)(2,1)S(1)}, u32[]{:S(2)}, u32[]{:S(2)}) collective-permute-start(bf16[1472,256]{1,0:T(8,128)(2,1)S(1)} %constant_dynamic-update-slice_fusion.1), channel_id=1, source_target_pairs={{0,1},{1,0},{2,3},{3,2},{4,5},{5,4},{6,7},{7,6},{8,9},{9,8},{10,11... | collective-permute-start | bytes 2261000 | tf_op jit(solution)/shard_map/ppermute | solution.py:273
